TPU v7x, 32 devices: a whole 2x2x4 slice. The times are simulated.
32 devices in a mesh: nets: 8 (over z, x), region: 4 (over y, core).
Axes of the slice: x: 2, y: 2, z: 4, core: 2. Of those that a mesh axis runs over, the one named last changes fastest.
Arguments:
- logits: float32 [8192, 256], P('nets'), may hold values from -24 to 465
- tile_values: bfloat16 [8, 4, 384, 128, 128], P('nets', 'region'), may hold values from 0 to 1
- tile_pattern: int32 [8, 4, 384], P('nets', 'region'), may hold values from 0 to 2047
- tile_edge: int32 [8, 4, 384], P('nets', 'region'), may hold values from 0 to 63
- tile_counts: int32 [8, 4, 8], P('nets', 'region'), may hold values from 12 to 48, as said below
- capacity: int32 [4, 65536], P('region', 'nets'), may hold values from 0 to 2
Outputs:
- logit_grad: float32 [8192, 256], P('nets')
- usage: float32 [4, 65536], P('region', 'nets')
Inputs may be any that keep to these rules, and one draw needn't show every extreme that they name: `tile_counts`: each entry is at most 48; in every draw some owner receives 48 live slots from every group of a region, and every group has a full owner in every region.
All inputs are finite; a program needn't handle non-finite values.
Results may differ from a plain program's by a relative error of at most 0.0011.
Values may be sent and summed in bfloat16 or wider, within the bound.
No kernel may reach another device: no remote copies, remote signals or barrier semaphores. Data moves between devices by JAX's collectives and lax.ppermute only.
A program may use at most 64 MiB of HBM per device.

v0:
```python
import jax
import jax.numpy as jnp
from jax import lax
from jax.sharding import PartitionSpec as P


def shards(logits, tile_values, tile_pattern, tile_edge, tile_counts, capacity):
    groups = lax.axis_size("nets")
    tile_block = tile_values[0, 0]
    tile_count = tile_block.shape[0]
    block_size = tile_block.shape[1]
    slot_count = tile_count // groups
    pattern_idx = tile_pattern[0, 0]
    edge_idx = tile_edge[0, 0]
    counts = tile_counts[0, 0]
    live_slot = (jnp.arange(slot_count, dtype=jnp.int32)[None, :] < counts[:, None]).reshape(
        tile_count
    )
    weight_live = live_slot.astype(jnp.float32)
    probs = jax.nn.softmax(logits, axis=-1)
    probs_half = probs.astype(jnp.bfloat16).reshape(-1, block_size)
    picked = probs_half[pattern_idx]
    contrib = (
        jnp.einsum("tq,tqe->te", picked, tile_block, preferred_element_type=jnp.float32)
        * weight_live[:, None]
    )
    capacity_f = capacity.reshape(-1, block_size).astype(jnp.float32)
    owned_blocks = capacity_f.shape[0]
    owner_idx = jnp.arange(tile_count, dtype=jnp.int32) // slot_count
    target = owner_idx * owned_blocks + edge_idx
    partial_value = (
        jnp.zeros((groups * owned_blocks, block_size), jnp.float32).at[target].add(contrib)
    )
    usage_edges = lax.psum_scatter(partial_value, "nets", scatter_dimension=0, tiled=True)
    edge_grad = jax.nn.sigmoid(usage_edges - capacity_f).astype(jnp.bfloat16)
    all_grads = lax.all_gather(edge_grad, "nets", axis=0, tiled=True)
    slot_grads = all_grads[target]
    dp_tiles = (
        jnp.einsum("tqe,te->tq", tile_block, slot_grads, preferred_element_type=jnp.float32)
        * weight_live[:, None]
    )
    local_grad = (
        jnp.zeros((probs_half.shape[0], block_size), jnp.float32).at[pattern_idx].add(dp_tiles)
    )
    summed_grad = lax.psum(local_grad.reshape(logits.shape), "region")
    logit_grad = probs * (summed_grad - jnp.sum(probs * summed_grad, axis=-1, keepdims=True))
    return (logit_grad, usage_edges.reshape(capacity.shape))


def solution(mesh):
    in_specs = (
        P("nets", None),
        P("nets", "region", None, None, None),
        P("nets", "region", None),
        P("nets", "region", None),
        P("nets", "region", None),
        P("region", "nets"),
    )
    out_specs = (P("nets", None), P("region", "nets"))
    return jax.shard_map(shards, mesh=mesh, in_specs=in_specs, out_specs=out_specs, check_vma=False)
```

profile of v0, /device:TPU:0, one launch (start us, length us, event | category | flops | bytes accessed | tf_op | source)
XLA Modules:
  0.0 181.0 jit_solution(4683535861114849851)
XLA Ops:
  7.2 0.0 reduce-scatter.2.cloned.1.call-start
  7.2 0.7 fusion.17
  7.9 0.7 fusion.18
  8.6 1.4 reduce_max.9
  10.1 1.6 fusion.5
  11.7 0.7 fusion.16
  12.4 0.1 reshape.122
  12.5 1.6 fusion.21
  14.0 0.0 copy-start.1
  14.1 0.2 reshape.119
  14.2 1.4 gather_fusion
  15.7 6.4 %fusion.2 = f32[384,1,128]{2,1,0:T(1,128)S(1)} fusion(bf16[1,1,384,128,128]{4,3,2,1,0:T(8,128)(2,1)} %param.7, bf16[384,128,1]{1,0,2:T(8,128)(2,1)S(1)} %bitcast.18), kind=kOutput, calls=%fused_computation.6 | convolution fusion | flops 12582912 | bytes 12877824 | tf_op jit(solution)/shard_map/tq,tqe->te/dot_general | solution.py:24
  22.1 0.0 copy-start
  22.1 2.6 %scatter_custom_fusion = f32[512,128]{1,0:T(8,128)} fusion(s32[384]{0:T(512)S(1)} %fusion.18, f32[384,128]{1,0:T(8,128)S(1)} %bitcast.19, f32[]{:T(128)} %constant.11.clone.1, f32[384]{0:T(512)S(1)} %reshape.122), kind=kCustom, calls=%fused_computation.18 | custom fusion | flops 98304 | bytes 460804 | tf_op jit(solution)/shard_map/scatter-add | solution.py:32
  24.7 0.0 reduce-scatter.2.cloned.1.call-update
  24.7 0.0 all-reduce.2.cloned.1.call-start
  24.8 0.0 copy-done.1
  24.8 64.0 %reduce-scatter.2.cloned.1.call-done = f32[64,128]{1,0:T(8,128)} async-done(((f32[512,128]{1,0:T(8,128)}), f32[64,128]{1,0:T(8,128)}) %reduce-scatter.2.cloned.1.call-update) | async-done | bytes 32784 | tf_op jit(solution)/shard_map/reduce_scatter | solution.py:34
  88.8 0.8 divide_convert_fusion
  89.6 30.5 %all_gather.3 = bf16[512,128]{1,0:T(8,128)(2,1)S(1)} all-gather(bf16[64,128]{1,0:T(8,128)(2,1)S(1)} %divide_convert_fusion), channel_id=1, replica_groups=mesh['nets'=8,'region'=4] {'nets'}, dimensions={0}, use_global_device_ids=true | all-gather | bytes 147456 | tf_op jit(solution)/shard_map/all_gather | solution.py:36
  120.1 1.4 gather_fusion.1
  121.6 9.5 %fusion = f32[384,1,128]{2,1,0:T(1,128)S(1)} fusion(bf16[1,1,384,128,128]{4,3,2,1,0:T(8,128)(2,1)} %param.7, bf16[384,128,1]{1,0,2:T(8,128)(2,1)S(1)} %bitcast.20), kind=kOutput, calls=%fused_computation.4 | convolution fusion | flops 12582912 | bytes 12877824 | tf_op jit(solution)/shard_map/tqe,te->tq/dot_general | solution.py:39
  131.0 2.2 %scatter_custom_fusion.1 = f32[2048,128]{1,0:T(8,128)S(1)} fusion(s32[384]{0:T(512)S(1)} %fusion.17, f32[]{:T(128)} %constant.11.clone.1, f32[384,128]{1,0:T(8,128)S(1)} %bitcast.21, f32[384]{0:T(512)S(1)} %reshape.122), kind=kCustom, calls=%fused_computation.13 | custom fusion | flops 98304 | bytes 1247236 | tf_op jit(solution)/shard_map/scatter-add | solution.py:43
  133.2 1.3 reshape.120
  134.5 0.0 all-reduce.2.cloned.1.call-update
  134.5 35.3 %all-reduce.2.cloned.1.call-done = f32[1024,256]{1,0:T(8,128)} async-done(((f32[1024,256]{1,0:T(8,128)}), f32[1024,256]{1,0:T(8,128)}) %all-reduce.2.cloned.1.call-update) | async-done | bytes 1048592 | tf_op jit(solution)/shard_map/psum | solution.py:45
  169.8 0.0 copy-done
  169.8 1.7 multiply_reduce_fusion
  171.5 2.7 %subtract_multiply_fusion = f32[1024,256]{1,0:T(8,128)} fusion(f32[1024,256]{1,0:T(8,128)} %all-reduce.2.cloned.1.call-done, f32[1024]{0:T(1024)S(1)} %multiply_reduce_fusion, f32[1024]{0:T(1024)S(1)} %fusion.5, f32[1024,256]{1,0:T(8,128)S(1)} %copy-done, f32[1024]{0:T(1024)S(1)} %reduce_max.9), kind=kLoop, calls=%fused_computation.8 | loop fusion | flops 1048576 | bytes 3158016 | tf_op jit(solution)/shard_map/mul | solution.py:46
  (3 shorter events, 0.0 us)
Async XLA Ops:
  7.2 81.6 %reduce-scatter.2.cloned.1.call-start = ((), (), s32[]{:S(2)}) async-start(), calls=%async_computation.1 | async-start | bytes 294912 | tf_op jit(solution)/shard_map/reduce_scatter | solution.py:34
  14.0 10.7 %copy-start.1 = (s32[1,8192]{1,0:T(1,128)S(1)}, s32[1,8192]{1,0:T(1,128)}, u32[]{:S(2)}) copy-start(s32[1,8192]{1,0:T(1,128)} %param.11) | copy-start | bytes 98308
  22.1 147.8 %copy-start = (f32[1024,256]{1,0:T(8,128)S(1)}, f32[1024,256]{1,0:T(8,128)}, u32[]{:S(2)}) copy-start(f32[1024,256]{1,0:T(8,128)} %param.6) | copy-start | bytes 3145732
  24.7 145.1 %all-reduce.2.cloned.1.call-start = ((), (), s32[]{:S(2)}) async-start(), calls=%async_computation.2 | async-start | bytes 2097152 | tf_op jit(solution)/shard_map/psum | solution.py:45
Sparse Core Ops, SparseCore 0:
  24.8 63.9 reduce-scatter.1
  134.7 35.0 all-reduce.1
where the time goes:
time: 181 us
  waiting for transfers between devices  99.3 us (55%)
  blocking collectives  30.5 us (17%)
  other arithmetic  16.8 us (9%)
  matrix products  15.8 us (9%)
  between operations  14.1 us (8%)
  local copies, waits for them, and re-layouts  4.42 us (2%)
    reduce_scatter x1, waiting for transfers between devices, shards(): lax.psum_scatter(partial_value, 'nets', scatter_dimension=0, tiled=True)  64 us
    psum x1, waiting for transfers between devices, shards(): summed_grad = lax.psum(local_grad.reshape(logits.shape), 'region')  35.3 us
    all_gather x1, blocking collectives, shards(): all_grads = lax.all_gather(edge_grad, 'nets', axis=0, tiled=True)  30.5 us
    dot_general x1, matrix products, shards(): jnp.einsum('tqe,te->tq', tile_block, slot_grads, preferred_element_type=j...  9.46 us
    dot_general x1, matrix products, shards(): jnp.einsum('tq,tqe->te', picked, tile_block, preferred_element_type=jnp.f...  6.35 us
  transfers between devices with their start and end apart: 2, of which 2 were waited for; matrix products, arithmetic and copies ran while one was open for 0% of the time, Pallas kernels for 0%

commit v1 on v0

--- a/solution.py
+++ b/solution.py
@@ -42,7 +42,7 @@
     local_grad = (
         jnp.zeros((probs_half.shape[0], block_size), jnp.float32).at[pattern_idx].add(dp_tiles)
     )
-    summed_grad = lax.psum(local_grad.reshape(logits.shape), "region")
+    summed_grad = jnp.sum(lax.all_gather(local_grad.reshape(logits.shape), "region"), axis=0)
     logit_grad = probs * (summed_grad - jnp.sum(probs * summed_grad, axis=-1, keepdims=True))
     return (logit_grad, usage_edges.reshape(capacity.shape))
 

time: 181 us -> 180 us (level)
    psum x1 -> x0, waiting for transfers between devices: 35.3 us -> none  [shards(): summed_grad = lax.psum(local_grad.reshape(logits.shape), 'region')]
    all_gather x0 -> x1, waiting for transfers between devices: none -> 33.7 us  [shards(): lax.all_gather(local_grad.reshape(logits.shape), 'region')]
    reduce_sum x0 -> x1, other arithmetic: none -> 2.59 us  [shards(): jnp.sum(lax.all_gather(local_grad.reshape(logits.shape), 'region'), axis=0)]
where the time goes in v1:
time: 180 us
  waiting for transfers between devices  97.7 us (54%)
  blocking collectives  30.5 us (17%)
  other arithmetic  16.9 us (9%)
  matrix products  15.8 us (9%)
  between operations  14.1 us (8%)
  local copies, waits for them, and re-layouts  4.42 us (2%)
    reduce_scatter x1, waiting for transfers between devices, shards(): lax.psum_scatter(partial_value, 'nets', scatter_dimension=0, tiled=True)  64 us
    all_gather x1, waiting for transfers between devices, shards(): lax.all_gather(local_grad.reshape(logits.shape), 'region')  33.7 us
    all_gather x1, blocking collectives, shards(): all_grads = lax.all_gather(edge_grad, 'nets', axis=0, tiled=True)  30.5 us
    dot_general x1, matrix products, shards(): jnp.einsum('tqe,te->tq', tile_block, slot_grads, preferred_element_type=j...  9.46 us
    dot_general x1, matrix products, shards(): jnp.einsum('tq,tqe->te', picked, tile_block, preferred_element_type=jnp.f...  6.35 us
  transfers between devices with their start and end apart: 2, of which 2 were waited for; matrix products, arithmetic and copies ran while one was open for 0% of the time, Pallas kernels for 0%

profile of v1, /device:TPU:0, one launch (start us, length us, event | category | flops | bytes accessed | tf_op | source)
XLA Modules:
  0.0 179.6 jit_solution(2664511002106358620)
XLA Ops:
  7.2 0.0 reduce-scatter.2.cloned.1.call-start
  7.2 0.7 fusion.17
  7.9 0.7 fusion.18
  8.6 1.4 reduce_max.9
  10.1 1.6 fusion.5
  11.7 0.7 fusion.16
  12.4 0.1 reshape.118
  12.5 1.6 fusion.21
  14.0 0.0 copy-start.1
  14.1 0.2 reshape.116
  14.2 1.4 gather_fusion
  15.7 6.4 %fusion.2 = f32[384,1,128]{2,1,0:T(1,128)S(1)} fusion(bf16[1,1,384,128,128]{4,3,2,1,0:T(8,128)(2,1)} %param.7, bf16[384,128,1]{1,0,2:T(8,128)(2,1)S(1)} %bitcast.18), kind=kOutput, calls=%fused_computation.6 | convolution fusion | flops 12582912 | bytes 12877824 | tf_op jit(solution)/shard_map/tq,tqe->te/dot_general | solution.py:24
  22.1 0.0 copy-start
  22.1 2.6 %scatter_custom_fusion = f32[512,128]{1,0:T(8,128)} fusion(s32[384]{0:T(512)S(1)} %fusion.18, f32[384,128]{1,0:T(8,128)S(1)} %bitcast.19, f32[]{:T(128)} %constant.11.clone.1, f32[384]{0:T(512)S(1)} %reshape.118), kind=kCustom, calls=%fused_computation.18 | custom fusion | flops 98304 | bytes 460804 | tf_op jit(solution)/shard_map/scatter-add | solution.py:32
  24.7 0.0 reduce-scatter.2.cloned.1.call-update
  24.7 0.0 all-gather.2.cloned.1.call-start
  24.8 0.0 copy-done.1
  24.8 64.0 %reduce-scatter.2.cloned.1.call-done = f32[64,128]{1,0:T(8,128)} async-done(((f32[512,128]{1,0:T(8,128)}), f32[64,128]{1,0:T(8,128)}) %reduce-scatter.2.cloned.1.call-update) | async-done | bytes 32784 | tf_op jit(solution)/shard_map/reduce_scatter | solution.py:34
  88.8 0.8 divide_convert_fusion
  89.6 30.5 %all_gather.6 = bf16[512,128]{1,0:T(8,128)(2,1)S(1)} all-gather(bf16[64,128]{1,0:T(8,128)(2,1)S(1)} %divide_convert_fusion), channel_id=1, replica_groups=mesh['nets'=8,'region'=4] {'nets'}, dimensions={0}, use_global_device_ids=true | all-gather | bytes 147456 | tf_op jit(solution)/shard_map/all_gather | solution.py:36
  120.1 1.4 gather_fusion.1
  121.6 9.5 %fusion = f32[384,1,128]{2,1,0:T(1,128)S(1)} fusion(bf16[1,1,384,128,128]{4,3,2,1,0:T(8,128)(2,1)} %param.7, bf16[384,128,1]{1,0,2:T(8,128)(2,1)S(1)} %bitcast.20), kind=kOutput, calls=%fused_computation.4 | convolution fusion | flops 12582912 | bytes 12877824 | tf_op jit(solution)/shard_map/tqe,te->tq/dot_general | solution.py:39
  131.0 2.2 %scatter_custom_fusion.1 = f32[2048,128]{1,0:T(8,128)S(1)} fusion(s32[384]{0:T(512)S(1)} %fusion.17, f32[]{:T(128)} %constant.11.clone.1, f32[384,128]{1,0:T(8,128)S(1)} %bitcast.21, f32[384]{0:T(512)S(1)} %reshape.118), kind=kCustom, calls=%fused_computation.13 | custom fusion | flops 98304 | bytes 1247236 | tf_op jit(solution)/shard_map/scatter-add | solution.py:43
  133.2 1.3 all_gather_reshape.3
  134.5 0.0 all-gather.2.cloned.1.call-update
  134.5 33.7 %all-gather.2.cloned.1.call-done = f32[4,1024,256]{2,1,0:T(8,128)} async-done(((f32[1,1024,256]{2,1,0:T(8,128)}), f32[4,1024,256]{2,1,0:T(8,128)}) %all-gather.2.cloned.1.call-update) | async-done | bytes 4194320 | tf_op jit(solution)/shard_map/all_gather | solution.py:45
  168.2 2.6 %reduce_sum.28 = f32[1024,256]{1,0:T(8,128)S(1)} reduce(f32[4,1024,256]{2,1,0:T(8,128)} %all-gather.2.cloned.1.call-done, f32[]{:T(128)} %constant.11.clone.1), dimensions={0}, to_apply=%region_5.6 | reduce | flops 786432 | bytes 5242884 | tf_op jit(solution)/shard_map/reduce_sum | solution.py:45
  170.8 0.0 copy-done
  170.8 0.5 multiply_reduce_fusion
  171.3 1.4 subtract_multiply_fusion
  (3 shorter events, 0.0 us)
Async XLA Ops:
  7.2 81.6 %reduce-scatter.2.cloned.1.call-start = ((), (), s32[]{:S(2)}) async-start(), calls=%async_computation.1 | async-start | bytes 294912 | tf_op jit(solution)/shard_map/reduce_scatter | solution.py:34
  14.0 10.7 %copy-start.1 = (s32[1,8192]{1,0:T(1,128)S(1)}, s32[1,8192]{1,0:T(1,128)}, u32[]{:S(2)}) copy-start(s32[1,8192]{1,0:T(1,128)} %param.11) | copy-start | bytes 98308
  22.1 148.8 %copy-start = (f32[1024,256]{1,0:T(8,128)S(1)}, f32[1024,256]{1,0:T(8,128)}, u32[]{:S(2)}) copy-start(f32[1024,256]{1,0:T(8,128)} %param.6) | copy-start | bytes 3145732
  24.7 143.5 %all-gather.2.cloned.1.call-start = ((), (), s32[]{:S(2)}) async-start(), calls=%async_computation.2 | async-start | bytes 5242880 | tf_op jit(solution)/shard_map/all_gather | solution.py:45
Sparse Core Ops, SparseCore 0:
  24.8 63.9 reduce-scatter.1
  134.7 33.5 all-gather.1
